TPU v7x, 32 devices: a whole 2x2x4 slice. The times are simulated.
32 devices in a mesh: feat: 8 (over y, x, core), tok: 4 (over z).
Axes of the slice: x: 2, y: 2, z: 4, core: 2. Of those that a mesh axis runs over, the one named last changes fastest.
Arguments:
- residual: bfloat16 [256, 4608], P('tok', 'feat'), may hold values from -700 to 700
- enc_weight: bfloat16 [4608, 8192], P(None, ('feat', 'tok')), may hold values from -0.09375 to 0.09375
- enc_bias: float32 [8192], P(('feat', 'tok')), may hold values from -3 to 3
- threshold: float32 [8192], P(('feat', 'tok')), may hold values from 0.25 to 2.5
- probe_weight: bfloat16 [8192, 16], P(('feat', 'tok')), may hold values from -0.375 to 0.375
- probe_bias: float32 [16], replicated, may hold values from -3 to 3
- labels: int32 [256], replicated, may hold values from 0 to 15
Outputs:
- probe_grad: float32 [8192, 16], P(('feat', 'tok'))
- token_loss: float32 [256], P(('feat', 'tok'))
All inputs are finite; a program needn't handle non-finite values.
Results may differ from a plain program's by a relative error of at most 0.0034.
Values may be sent and summed in bfloat16 or wider, within the bound.
No kernel may reach another device: no remote copies, remote signals or barrier semaphores. Data moves between devices by JAX's collectives and lax.ppermute only.
A program may use at most 64 MiB of HBM per device.

v0:
```python
import jax
import jax.numpy as jnp
from jax import lax
from jax.sharding import PartitionSpec as P

epsilon = 1e-06
smooth_width = 0.125


def normalize(values, squares):
    full_width = values.shape[1] * lax.axis_size("feat")
    row_scale = lax.rsqrt(squares / full_width + epsilon)
    return (values * row_scale[:, None]).astype(jnp.bfloat16)


def local(residual, enc_weight, enc_bias, threshold, probe_weight, probe_bias, labels):
    values = residual.astype(jnp.float32)
    squares = lax.psum(jnp.sum(values * values, axis=1), "feat")
    normed = normalize(values, squares)
    all_tokens = lax.all_gather(normed, "tok", axis=0, tiled=True)
    preact = jnp.dot(
        lax.all_gather(all_tokens, "feat", axis=1, tiled=True),
        enc_weight,
        preferred_element_type=jnp.float32,
    )
    encode_preact = preact
    encode_preact = encode_preact + enc_bias
    features = (encode_preact * jax.nn.sigmoid((encode_preact - threshold) / smooth_width)).astype(
        jnp.bfloat16
    )
    partial_value = jnp.dot(features, probe_weight, preferred_element_type=jnp.float32)
    num_tokens = features.shape[0]
    share_rows = num_tokens // lax.axis_size(("feat", "tok"))
    position = lax.axis_index(("feat", "tok"))
    class_ids = jnp.arange(probe_weight.shape[1], dtype=jnp.int32)
    logits = lax.psum(partial_value, ("feat", "tok"))
    softmax_logits = logits
    softmax_logits = softmax_logits + probe_bias
    exps = jnp.exp(softmax_logits)
    totals = jnp.sum(exps, axis=1, keepdims=True)
    onehot = (labels[:, None] == class_ids[None, :]).astype(jnp.float32)
    losses = jnp.log(totals[:, 0]) - jnp.sum(onehot * softmax_logits, axis=1)
    losses, delta = (losses, (exps / totals - onehot).astype(jnp.bfloat16))
    token_loss = lax.dynamic_slice_in_dim(losses, position * share_rows, share_rows, 0)
    gradient = jnp.dot(features.T, delta, preferred_element_type=jnp.float32)
    return (gradient, token_loss)


def solution(mesh):
    in_specs = (
        P("tok", "feat"),
        P(None, ("feat", "tok")),
        P(("feat", "tok")),
        P(("feat", "tok")),
        P(("feat", "tok"), None),
        P(),
        P(),
    )
    out_specs = (P(("feat", "tok"), None), P(("feat", "tok")))
    return jax.shard_map(local, mesh=mesh, in_specs=in_specs, out_specs=out_specs, check_vma=False)
```

profile of v0, /device:TPU:0, one launch (start us, length us, event | category | flops | bytes accessed | tf_op | source)
XLA Modules:
  0.0 118.5 jit_solution(7145613870447156144)
XLA Ops:
  7.2 0.0 copy-start
  7.2 0.0 all-gather.2.cloned.1.call-start
  7.2 1.2 fusion
  8.4 15.2 %psum.14 = f32[64]{0:T(128)S(1)} all-reduce(f32[64]{0:T(128)S(1)} %fusion), channel_id=1, replica_groups=mesh['feat'=8,'tok'=4] {'feat'}, use_global_device_ids=true, to_apply=%region_1.0 | all-reduce | flops 64 | bytes 512 | tf_op jit(solution)/shard_map/psum | solution.py:18
  23.5 1.0 fusion.1
  24.5 14.9 %all_gather.6 = bf16[256,576]{1,0:T(8,128)(2,1)S(1)} all-gather(bf16[64,576]{1,0:T(8,128)(2,1)S(1)} %fusion.1), channel_id=1, replica_groups=mesh['feat'=8,'tok'=4] {'tok'}, dimensions={0}, use_global_device_ids=true | all-gather | bytes 368640 | tf_op jit(solution)/shard_map/all_gather | solution.py:20
  39.4 0.9 copy.10
  40.3 0.0 all-gather.2.cloned.1.call-update
  40.3 0.0 copy-start.1
  40.3 0.0 copy-start.2
  40.4 0.0 copy-start.3
  40.4 27.8 %all-gather.2.cloned.1.call-done = bf16[256,4608]{0,1:T(8,128)(2,1)} async-done(((bf16[256,576]{0,1:T(8,128)(2,1)}), bf16[256,4608]{0,1:T(8,128)(2,1)}) %all-gather.2.cloned.1.call-update) | async-done | bytes 2359312 | tf_op jit(solution)/shard_map/all_gather | solution.py:22
  68.1 0.0 copy-done
  68.1 2.5 %multiply_convert_fusion = bf16[256,256]{1,0:T(8,128)(2,1)S(1)} fusion(bf16[256,4608]{0,1:T(8,128)(2,1)} %all-gather.2.cloned.1.call-done, bf16[4608,256]{1,0:T(8,128)(2,1)S(1)} %copy-done, f32[256]{0:T(256)} %param.10, f32[256]{0:T(256)} %param.9), kind=kOutput, calls=%fused_computation.1 | convolution fusion | flops 604504064 | bytes 4851712 | tf_op jit(solution)/shard_map/dot_general | solution.py:21
  70.7 0.0 copy-done.1
  70.7 0.1 fusion.6
  70.8 39.3 %psum.15 = f32[256,16]{0,1:T(8,128)S(1)} all-reduce(f32[256,16]{0,1:T(8,128)S(1)} %fusion.6), channel_id=1, replica_groups=mesh['feat'=8,'tok'=4] {'feat','tok'}, use_global_device_ids=true, to_apply=%region_2.0 | all-reduce | flops 4096 | bytes 32768 | tf_op jit(solution)/shard_map/psum | solution.py:36
  110.2 0.0 copy-done.2
  110.2 0.0 copy-done.3
  110.2 0.1 select_reduce_fusion
  110.3 0.8 fusion.2
  111.1 0.6 dynamic_slice.3
  (2 shorter events, 0.0 us)
Async XLA Ops:
  7.2 61.0 %copy-start = (bf16[4608,256]{1,0:T(8,128)(2,1)S(1)}, bf16[4608,256]{1,0:T(8,128)(2,1)}, u32[]{:S(2)}) copy-start(bf16[4608,256]{1,0:T(8,128)(2,1)} %param.8) | copy-start | bytes 7077892
  7.2 60.9 %all-gather.2.cloned.1.call-start = ((), (), s32[]{:S(2)}) async-start(), calls=%async_computation | async-start | bytes 2654208 | tf_op jit(solution)/shard_map/all_gather | solution.py:22
  40.3 30.3 %copy-start.1 = (bf16[256,16]{0,1:T(8,128)(2,1)S(1)}, bf16[256,16]{0,1:T(8,128)(2,1)}, u32[]{:S(2)}) copy-start(bf16[256,16]{0,1:T(8,128)(2,1)} %param.11) | copy-start | bytes 24580
  40.3 69.8 %copy-start.2 = (s32[256]{0:T(256)S(1)}, s32[256]{0:T(256)}, u32[]{:S(2)}) copy-start(s32[256]{0:T(256)} %param.13) | copy-start | bytes 3076
  40.4 69.8 %copy-start.3 = (f32[16]{0:T(128)S(1)}, f32[16]{0:T(128)}, u32[]{:S(2)}) copy-start(f32[16]{0:T(128)} %param.12) | copy-start | bytes 196
Sparse Core Ops, SparseCore 0:
  40.5 27.6 all-gather.1
where the time goes:
time: 119 us
  blocking collectives  69.4 us (58%)
  waiting for transfers between devices  27.8 us (23%)
  between operations  14.1 us (12%)
  matrix products  3.49 us (3%)
  other arithmetic  2.24 us (2%)
  local copies, waits for them, and re-layouts  1.5 us (1%)
    psum x1, blocking collectives, local(): logits = lax.psum(partial_value, ('feat', 'tok'))  39.3 us
    all_gather x1, waiting for transfers between devices, local(): lax.all_gather(all_tokens, 'feat', axis=1, tiled=True)  27.8 us
    psum x1, blocking collectives, local(): squares = lax.psum(jnp.sum(values * values, axis=1), 'feat')  15.2 us
    all_gather x1, blocking collectives, local(): all_tokens = lax.all_gather(normed, 'tok', axis=0, tiled=True)  14.9 us
    dot_general x1, matrix products, local(): jnp.dot(lax.all_gather(all_tokens, 'feat', axis=1, tiled=True), enc_weigh...  2.53 us
  transfers between devices with their start and end apart: 1, of which 1 were waited for; matrix products, arithmetic and copies ran while one was open for 0% of the time, Pallas kernels for 0%

commit v1 on v0

v1 whole, which is shorter than its diff:
```python
import jax
import jax.numpy as jnp
from jax import lax
from jax.sharding import PartitionSpec as P

epsilon = 1e-06
smooth_width = 0.125


def bits_of(n):
    count = n.bit_length() - 1
    assert 1 << count == n
    return count


def exchange(value, axis, bit):
    size = lax.axis_size(axis)
    return lax.ppermute(value, axis, [(i, i ^ (1 << bit)) for i in range(size)])


def gather_steps():
    tok_bits = bits_of(lax.axis_size("tok"))
    feat_bits = bits_of(lax.axis_size("feat"))
    steps = [("tok", b) for b in reversed(range(tok_bits))]
    steps += [("feat", b) for b in range(1, feat_bits)] + [("feat", 0)]
    return steps


def gather_all(block, steps):
    rows, cols = block.shape
    held = block
    done = {"tok": [], "feat": []}
    for axis, bit in steps:
        other = exchange(held, axis, bit)
        mine = (lax.axis_index(axis) >> bit) & 1
        low = jnp.where(mine == 0, held, other)
        high = jnp.where(mine == 0, other, held)
        above = sum(1 for b in done[axis] if b > bit)
        start = 0 if axis == "tok" else len(done["tok"]) + 1
        held = jnp.stack([low, high], axis=start + above)
        done[axis].append(bit)
    return held, len(done["tok"])


def reduce_all(value, steps):
    for axis, bit in steps:
        value = value + exchange(value, axis, bit)
    return value


def local(residual, enc_weight, enc_bias, threshold, probe_weight, probe_bias, labels):
    steps = gather_steps()
    held, tok_dims = gather_all(residual, steps)
    held = lax.optimization_barrier(held)
    values = held.astype(jnp.float32)
    width_axes = tuple(range(tok_dims + 1, held.ndim))
    full_width = residual.shape[1] * lax.axis_size("feat")
    mean_square = jnp.sum(values * values, axis=width_axes, keepdims=True) / full_width
    normed = (values * lax.rsqrt(mean_square + epsilon)).astype(jnp.bfloat16)
    normed = normed.reshape(residual.shape[0] * lax.axis_size("tok"), full_width)
    preact = jnp.dot(normed, enc_weight, preferred_element_type=jnp.float32)
    encode_preact = preact + enc_bias
    features = (encode_preact * jax.nn.sigmoid((encode_preact - threshold) / smooth_width)).astype(
        jnp.bfloat16
    )
    partial_value = jnp.dot(features, probe_weight, preferred_element_type=jnp.float32)
    num_tokens = features.shape[0]
    share_rows = num_tokens // lax.axis_size(("feat", "tok"))
    position = lax.axis_index(("feat", "tok"))
    class_ids = jnp.arange(probe_weight.shape[1], dtype=jnp.int32)
    logits = reduce_all(partial_value, steps)
    softmax_logits = logits + probe_bias
    exps = jnp.exp(softmax_logits)
    totals = jnp.sum(exps, axis=1, keepdims=True)
    onehot = (labels[:, None] == class_ids[None, :]).astype(jnp.float32)
    losses = jnp.log(totals[:, 0]) - jnp.sum(onehot * softmax_logits, axis=1)
    delta = (exps / totals - onehot).astype(jnp.bfloat16)
    token_loss = lax.dynamic_slice_in_dim(losses, position * share_rows, share_rows, 0)
    gradient = jnp.dot(features.T, delta, preferred_element_type=jnp.float32)
    return (gradient, token_loss)


def solution(mesh):
    in_specs = (
        P("tok", "feat"),
        P(None, ("feat", "tok")),
        P(("feat", "tok")),
        P(("feat", "tok")),
        P(("feat", "tok"), None),
        P(),
        P(),
    )
    out_specs = (P(("feat", "tok"), None), P(("feat", "tok")))
    return jax.shard_map(local, mesh=mesh, in_specs=in_specs, out_specs=out_specs, check_vma=False)
```

time: 119 us -> 86 us (0.72)
  blocking collectives: 69.4 us -> 0 us
  starting transfers between devices: 0.04 us -> 18 us
  between operations: 14.1 us -> 0.77 us
  waiting for transfers between devices: 27.8 us -> 40.9 us
  local copies, waits for them, and re-layouts: 1.5 us -> 13.9 us
  other arithmetic: 2.24 us -> 8.67 us
    psum x2 -> x0, blocking collectives: 54.5 us -> none  [the longest x1 39.3 us: local(): logits = lax.psum(partial_value, ('feat', 'tok'))]
    ppermute x0 -> x10, waiting for transfers between devices: none -> 40.9 us  [exchange(): return lax.ppermute(value, axis, [(i, i ^ 1 << bit) for i in range(size)])]
    all_gather x1 -> x0, waiting for transfers between devices: 27.8 us -> none  [local(): lax.all_gather(all_tokens, 'feat', axis=1, tiled=True)]
    ppermute x0 -> x10, starting transfers between devices: none -> 18 us  [exchange(): return lax.ppermute(value, axis, [(i, i ^ 1 << bit) for i in range(size)])]
    all_gather x1 -> x0, blocking collectives: 14.9 us -> none  [local(): all_tokens = lax.all_gather(normed, 'tok', axis=0, tiled=True)]
    reshape x0 -> x1, local copies, waits for them, and re-layouts: none -> 7.55 us  [local(): normed.reshape(residual.shape[0] * lax.axis_size('tok'), full_width)]
    another operation x0 -> x10, other arithmetic: none -> 7.03 us  [gather_all(): held = jnp.stack([low, high], axis=start + above)]
    convert_element_type x0 -> x1, local copies, waits for them, and re-layouts: none -> 4.2 us  [local(): normed = (values * lax.rsqrt(mean_square + epsilon)).astype(jnp.bfloat16)]
  transfers between devices with their start and end apart: 1 -> 10, of which waited for: 1 -> 10; matrix products, arithmetic and copies ran while one was open for 0% -> 0% of each run, Pallas kernels for 0% -> 0%
where the time goes in v1:
time: 86 us; the launch traced here: 85.7 us
  waiting for transfers between devices  40.9 us (48%)
  starting transfers between devices  18 us (21%)
  local copies, waits for them, and re-layouts  13.9 us (16%)
  other arithmetic  8.67 us (10%)
  matrix products  3.39 us (4%)
    ppermute x10, waiting for transfers between devices, exchange(): return lax.ppermute(value, axis, [(i, i ^ 1 << bit) for i in range(size)])  40.9 us
    ppermute x10, starting transfers between devices, exchange(): return lax.ppermute(value, axis, [(i, i ^ 1 << bit) for i in range(size)])  18 us
    reshape x1, local copies, waits for them, and re-layouts, local(): normed.reshape(residual.shape[0] * lax.axis_size('tok'), full_width)  7.55 us
    another operation x10, other arithmetic, gather_all(): held = jnp.stack([low, high], axis=start + above)  7.03 us
    convert_element_type x1, local copies, waits for them, and re-layouts, local(): normed = (values * lax.rsqrt(mean_square + epsilon)).astype(jnp.bfloat16)  4.2 us
    dot_general x1, matrix products, local(): preact = jnp.dot(normed, enc_weight, preferred_element_type=jnp.float32)  2.48 us
  transfers between devices with their start and end apart: 10, of which 10 were waited for; matrix products, arithmetic and copies ran while one was open for 0% of the time, Pallas kernels for 0%

profile of v1, /device:TPU:0, one launch (start us, length us, event | category | flops | bytes accessed | tf_op | source)
XLA Modules:
  0.0 85.7 jit_solution(2329912302995176007)
XLA Ops:
  0.6 4.1 %collective-permute-start = (bf16[64,576]{1,0:T(8,128)(2,1)}, bf16[64,576]{1,0:T(8,128)(2,1)S(1)}, u32[]{:S(2)}, u32[]{:S(2)}) collective-permute-start(bf16[64,576]{1,0:T(8,128)(2,1)} %param.7), channel_id=1, source_target_pairs={{0,2},{1,3},{2,0},{3,1},{4,6},{5,7},{6,4},{7,5},{8,10},{9,11},{10,... | collective-permute-start | bytes 221192 | tf_op jit(solution)/shard_map/ppermute | solution.py:18
  4.8 4.4 %collective-permute-done = bf16[64,576]{1,0:T(8,128)(2,1)S(1)} collective-permute-done((bf16[64,576]{1,0:T(8,128)(2,1)}, bf16[64,576]{1,0:T(8,128)(2,1)S(1)}, u32[]{:S(2)}, u32[]{:S(2)}) %collective-permute-start) | collective-permute-done | bytes 73760 | tf_op jit(solution)/shard_map/ppermute | solution.py:18
  11.0 4.5 %collective-permute-done.1 = bf16[2,64,576]{2,1,0:T(8,128)(2,1)S(1)} collective-permute-done((bf16[2,64,576]{2,1,0:T(8,128)(2,1)S(1)}, bf16[2,64,576]{2,1,0:T(8,128)(2,1)S(1)}, u32[]{:S(2)}, u32[]{:S(2)}) %collective-permute-start.1) | collective-permute-done | bytes 147488 | tf_op jit(solution)/shard_map/ppermute | solution.py:18
  15.6 1.7 %collective-permute-start.2 = (bf16[2,2,64,576]{3,2,0,1:T(8,128)(2,1)S(1)}, bf16[2,2,64,576]{3,2,0,1:T(8,128)(2,1)}, u32[]{:S(2)}, u32[]{:S(2)}) collective-permute-start(bf16[2,2,64,576]{3,2,0,1:T(8,128)(2,1)S(1)} %pad_maximum_fusion.3), channel_id=1, source_target_pairs={{0,8},{4,12},{8,0},{12,4},{16,24},{20,28},{24,16},{28,20},{1,9},{5... | collective-permute-start | bytes 884744 | tf_op jit(solution)/shard_map/ppermute | solution.py:18
  17.4 6.0 %collective-permute-done.2 = bf16[2,2,64,576]{3,2,0,1:T(8,128)(2,1)} collective-permute-done((bf16[2,2,64,576]{3,2,0,1:T(8,128)(2,1)S(1)}, bf16[2,2,64,576]{3,2,0,1:T(8,128)(2,1)}, u32[]{:S(2)}, u32[]{:S(2)}) %collective-permute-start.2) | collective-permute-done | bytes 294944 | tf_op jit(solution)/shard_map/ppermute | solution.py:18
  23.4 1.1 %select_bitcast_fusion.5 = (bf16[2,2,64,1,576]{4,2,0,1,3:T(8,128)(2,1)S(1)}, bf16[2,2,64,1,576]{4,2,0,1,3:T(8,128)(2,1)S(1)}) fusion(bf16[2,2,64,576]{3,2,0,1:T(8,128)(2,1)} %collective-permute-done.2, pred[]{:T(512)S(6)} %eq.35, bf16[2,1,64,576]{3,2,0,1:T(8,128)(2,1)S(1)} %get-tuple-element.12, bf16[2,1,64,576]{3,2,0,1:T(8,128)(2,1)S(1)} %get-tuple-element.11), kind=kLoop, calls=%fused_computation.14 | loop fusion | flops 442368 | bytes 1179649 | tf_op jit(solution)/shard_map/stack | solution.py:40
  25.3 1.6 %collective-permute-start.3 = (bf16[2,2,64,2,576]{4,2,0,1,3:T(8,128)(2,1)S(1)}, bf16[2,2,64,2,576]{4,2,0,1,3:T(8,128)(2,1)}, u32[]{:S(2)}, u32[]{:S(2)}) collective-permute-start(bf16[2,2,64,2,576]{4,2,0,1,3:T(8,128)(2,1)S(1)} %pad_maximum_fusion.2), channel_id=1, source_target_pairs={{0,16},{4,20},{8,24},{12,28},{16,0},{20,4},{24,8},{28,12},{1,17},{... | collective-permute-start | bytes 1769480 | tf_op jit(solution)/shard_map/ppermute | solution.py:18
  26.9 12.4 %collective-permute-done.3 = bf16[2,2,64,2,576]{4,2,0,1,3:T(8,128)(2,1)} collective-permute-done((bf16[2,2,64,2,576]{4,2,0,1,3:T(8,128)(2,1)S(1)}, bf16[2,2,64,2,576]{4,2,0,1,3:T(8,128)(2,1)}, u32[]{:S(2)}, u32[]{:S(2)}) %collective-permute-start.3) | collective-permute-done | bytes 589856 | tf_op jit(solution)/shard_map/ppermute | solution.py:18
  39.2 1.3 %select_bitcast_fusion.3 = (bf16[2,2,64,1,2,576]{5,2,0,1,4,3:T(8,128)(2,1)S(1)}, bf16[2,2,64,1,2,576]{5,2,0,1,4,3:T(8,128)(2,1)S(1)}) fusion(bf16[2,2,64,2,576]{4,2,0,1,3:T(8,128)(2,1)} %collective-permute-done.3, pred[]{:T(512)S(6)} %eq.34, bf16[2,2,64,1,576]{4,2,0,1,3:T(8,128)(2,1)} %copy-done.2, bf16[2,2,64,1,576]{4,2,0,1,3:T(8,128)(2,1)S(1)} %get-tuple-element.9), kind=kLoop, calls=%fused_computation.11 | loop fusion | flops 884736 | bytes 2359297 | tf_op jit(solution)/shard_map/stack | solution.py:40
  41.4 1.3 %pad_maximum_fusion.1 = bf16[2,2,64,2,2,576]{5,2,0,1,4,3:T(8,128)(2,1)} fusion(bf16[2,2,64,1,2,576]{5,2,0,1,4,3:T(8,128)(2,1)S(1)} %get-tuple-element.8, bf16[2,2,64,1,2,576]{5,2,0,1,4,3:T(8,128)(2,1)S(1)} %get-tuple-element.7), kind=kLoop, calls=%fused_computation.5 | loop fusion | flops 589824 | bytes 2359296 | tf_op jit(solution)/shard_map/stack | solution.py:40
  42.7 3.4 %collective-permute-done.4 = bf16[2,2,64,2,2,576]{5,2,0,1,4,3:T(8,128)(2,1)} collective-permute-done((bf16[2,2,64,2,2,576]{5,2,0,1,4,3:T(8,128)(2,1)}, bf16[2,2,64,2,2,576]{5,2,0,1,4,3:T(8,128)(2,1)}, u32[]{:S(2)}, u32[]{:S(2)}) %collective-permute-start.4) | collective-permute-done | bytes 1179680 | tf_op jit(solution)/shard_map/ppermute | solution.py:18
  46.1 1.8 %select_bitcast_fusion.1 = (bf16[2,2,64,2,2,1,576]{6,2,0,1,4,3,5:T(8,128)(2,1)S(1)}, bf16[2,2,64,2,2,1,576]{6,2,0,1,4,3,5:T(8,128)(2,1)S(1)}) fusion(bf16[2,2,64,2,2,576]{5,2,0,1,4,3:T(8,128)(2,1)} %collective-permute-done.4, pred[]{:T(512)S(6)} %eq.16, bf16[2,2,64,1,2,576]{5,2,0,1,4,3:T(8,128)(2,1)} %copy-done.1, ...), kind=kLoop, calls=%fused_computation.7 | loop fusion | flops 1769472 | bytes 4718593 | tf_op jit(solution)/shard_map/stack | solution.py:40
  49.8 4.2 %copy.9 = bf16[2,2,64,2,2,2,576]{6,5,4,3,2,1,0:T(2,128)(2,1)} copy(bf16[2,2,64,2,2,2,576]{6,2,0,1,4,3,5:T(8,128)(2,1)S(1)} %fusion.1) | data formatting | bytes 4718592 | tf_op jit(solution)/shard_map/convert_element_type | solution.py:59
  54.0 7.5 %reshape.20 = bf16[256,4608]{1,0:T(8,128)(2,1)} reshape(bf16[2,2,64,2,2,2,576]{6,5,4,3,2,1,0:T(2,128)(2,1)} %copy.9) | data formatting | bytes 4718592 | tf_op jit(solution)/shard_map/reshape | solution.py:60
  61.6 2.5 %multiply_convert_fusion = bf16[256,256]{1,0:T(8,128)(2,1)S(1)} fusion(bf16[256,4608]{1,0:T(8,128)(2,1)} %reshape.20, bf16[4608,256]{1,0:T(8,128)(2,1)S(1)} %copy-done, f32[256]{0:T(256)S(1)} %copy-done.6, f32[256]{0:T(256)S(1)} %copy-done.7), kind=kOutput, calls=%fused_computation.15 | convolution fusion | flops 604504064 | bytes 4851712 | tf_op jit(solution)/shard_map/dot_general | solution.py:61
  64.3 5.6 %collective-permute-start.5 = (f32[256,16]{0,1:T(8,128)S(1)}, f32[256,16]{0,1:T(8,128)S(1)}, u32[]{:S(2)}, u32[]{:S(2)}) collective-permute-start(f32[256,16]{0,1:T(8,128)S(1)} %fusion.5), channel_id=1, source_target_pairs={{0,2},{1,3},{2,0},{3,1},{4,6},{5,7},{6,4},{7,5},{8,10},{9,11},{10,... | collective-permute-start | bytes 49160 | tf_op jit(solution)/shard_map/ppermute | solution.py:18
  69.9 1.9 %collective-permute-done.5 = f32[256,16]{0,1:T(8,128)S(1)} collective-permute-done((f32[256,16]{0,1:T(8,128)S(1)}, f32[256,16]{0,1:T(8,128)S(1)}, u32[]{:S(2)}, u32[]{:S(2)}) %collective-permute-start.5) | collective-permute-done | bytes 16416 | tf_op jit(solution)/shard_map/ppermute | solution.py:18
  71.8 1.0 %collective-permute-start.6 = (f32[256,16]{0,1:T(8,128)S(1)}, f32[256,16]{0,1:T(8,128)S(1)}, u32[]{:S(2)}, u32[]{:S(2)}) collective-permute-start(f32[256,16]{0,1:T(8,128)S(1)} %add.56), channel_id=1, source_target_pairs={{0,1},{1,0},{2,3},{3,2},{4,5},{5,4},{6,7},{7,6},{8,9},{9,8},{10,11... | collective-permute-start | bytes 49160 | tf_op jit(solution)/shard_map/ppermute | solution.py:18
  72.8 2.7 %collective-permute-done.6 = f32[256,16]{0,1:T(8,128)S(1)} collective-permute-done((f32[256,16]{0,1:T(8,128)S(1)}, f32[256,16]{0,1:T(8,128)S(1)}, u32[]{:S(2)}, u32[]{:S(2)}) %collective-permute-start.6) | collective-permute-done | bytes 16416 | tf_op jit(solution)/shard_map/ppermute | solution.py:18
  75.5 1.5 %collective-permute-start.7 = (f32[256,16]{0,1:T(8,128)S(1)}, f32[256,16]{0,1:T(8,128)S(1)}, u32[]{:S(2)}, u32[]{:S(2)}) collective-permute-start(f32[256,16]{0,1:T(8,128)S(1)} %add.57), channel_id=1, source_target_pairs={{0,8},{4,12},{8,0},{12,4},{16,24},{20,28},{24,16},{28,20},{1,9},{5... | collective-permute-start | bytes 49160 | tf_op jit(solution)/shard_map/ppermute | solution.py:18
  77.0 2.2 %collective-permute-done.7 = f32[256,16]{0,1:T(8,128)S(1)} collective-permute-done((f32[256,16]{0,1:T(8,128)S(1)}, f32[256,16]{0,1:T(8,128)S(1)}, u32[]{:S(2)}, u32[]{:S(2)}) %collective-permute-start.7) | collective-permute-done | bytes 16416 | tf_op jit(solution)/shard_map/ppermute | solution.py:18
  79.3 1.5 %collective-permute-start.8 = (f32[256,16]{0,1:T(8,128)S(1)}, f32[256,16]{0,1:T(8,128)S(1)}, u32[]{:S(2)}, u32[]{:S(2)}) collective-permute-start(f32[256,16]{0,1:T(8,128)S(1)} %add.58), channel_id=1, source_target_pairs={{0,16},{4,20},{8,24},{12,28},{16,0},{20,4},{24,8},{28,12},{1,17},{... | collective-permute-start | bytes 49160 | tf_op jit(solution)/shard_map/ppermute | solution.py:18
  80.8 2.2 %collective-permute-done.8 = f32[256,16]{0,1:T(8,128)S(1)} collective-permute-done((f32[256,16]{0,1:T(8,128)S(1)}, f32[256,16]{0,1:T(8,128)S(1)}, u32[]{:S(2)}, u32[]{:S(2)}) %collective-permute-start.8) | collective-permute-done | bytes 16416 | tf_op jit(solution)/shard_map/ppermute | solution.py:18
  83.0 1.2 %collective-permute-done.9 = f32[256,16]{0,1:T(8,128)S(1)} collective-permute-done((f32[256,16]{0,1:T(8,128)S(1)}, f32[256,16]{0,1:T(8,128)S(1)}, u32[]{:S(2)}, u32[]{:S(2)}) %collective-permute-start.9) | collective-permute-done | bytes 16416 | tf_op jit(solution)/shard_map/ppermute | solution.py:18
  (37 shorter events, 7.1 us)
Async XLA Ops:
  0.6 61.0 %copy-start = (bf16[4608,256]{1,0:T(8,128)(2,1)S(1)}, bf16[4608,256]{1,0:T(8,128)(2,1)}, u32[]{:S(2)}) copy-start(bf16[4608,256]{1,0:T(8,128)(2,1)} %param.8) | copy-start | bytes 7077892
  0.6 8.5 %collective-permute-start = (bf16[64,576]{1,0:T(8,128)(2,1)}, bf16[64,576]{1,0:T(8,128)(2,1)S(1)}, u32[]{:S(2)}, u32[]{:S(2)}) collective-permute-start(bf16[64,576]{1,0:T(8,128)(2,1)} %param.7), channel_id=1, source_target_pairs={{0,2},{1,3},{2,0},{3,1},{4,6},{5,7},{6,4},{7,5},{8,10},{9,11},{10,... | collective-permute-start | bytes 221192 | tf_op jit(solution)/shard_map/ppermute | solution.py:18
  10.1 5.4 %collective-permute-start.1 = (bf16[2,64,576]{2,1,0:T(8,128)(2,1)S(1)}, bf16[2,64,576]{2,1,0:T(8,128)(2,1)S(1)}, u32[]{:S(2)}, u32[]{:S(2)}) collective-permute-start(bf16[2,64,576]{2,1,0:T(8,128)(2,1)S(1)} %pad_maximum_fusion.4), channel_id=1, source_target_pairs={{0,1},{1,0},{2,3},{3,2},{4,5},{5,4},{6,7},{7,6},{8,9},{9,8},{10,11... | collective-permute-start | bytes 442376 | tf_op jit(solution)/shard_map/ppermute | solution.py:18
  15.6 7.8 %collective-permute-start.2 = (bf16[2,2,64,576]{3,2,0,1:T(8,128)(2,1)S(1)}, bf16[2,2,64,576]{3,2,0,1:T(8,128)(2,1)}, u32[]{:S(2)}, u32[]{:S(2)}) collective-permute-start(bf16[2,2,64,576]{3,2,0,1:T(8,128)(2,1)S(1)} %pad_maximum_fusion.3), channel_id=1, source_target_pairs={{0,8},{4,12},{8,0},{12,4},{16,24},{20,28},{24,16},{28,20},{1,9},{5... | collective-permute-start | bytes 884744 | tf_op jit(solution)/shard_map/ppermute | solution.py:18
  24.5 0.7 copy-start.2
  25.3 13.9 %collective-permute-start.3 = (bf16[2,2,64,2,576]{4,2,0,1,3:T(8,128)(2,1)S(1)}, bf16[2,2,64,2,576]{4,2,0,1,3:T(8,128)(2,1)}, u32[]{:S(2)}, u32[]{:S(2)}) collective-permute-start(bf16[2,2,64,2,576]{4,2,0,1,3:T(8,128)(2,1)S(1)} %pad_maximum_fusion.2), channel_id=1, source_target_pairs={{0,16},{4,20},{8,24},{12,28},{16,0},{20,4},{24,8},{28,12},{1,17},{... | collective-permute-start | bytes 1769480 | tf_op jit(solution)/shard_map/ppermute | solution.py:18
  40.6 0.8 copy-start.1
  42.7 3.4 %collective-permute-start.4 = (bf16[2,2,64,2,2,576]{5,2,0,1,4,3:T(8,128)(2,1)}, bf16[2,2,64,2,2,576]{5,2,0,1,4,3:T(8,128)(2,1)}, u32[]{:S(2)}, u32[]{:S(2)}) collective-permute-start(bf16[2,2,64,2,2,576]{5,2,0,1,4,3:T(8,128)(2,1)} %pad_maximum_fusion.1), channel_id=1, source_target_pairs={{0,4},{4,0},{8,12},{12,8},{16,20},{20,16},{24,28},{28,24},{1,5},{5... | collective-permute-start | bytes 3538952 | tf_op jit(solution)/shard_map/ppermute | solution.py:18
  54.0 7.6 %copy-start.6 = (f32[256]{0:T(256)S(1)}, f32[256]{0:T(256)}, u32[]{:S(2)}) copy-start(f32[256]{0:T(256)} %param.10) | copy-start | bytes 3076
  54.0 7.6 %copy-start.7 = (f32[256]{0:T(256)S(1)}, f32[256]{0:T(256)}, u32[]{:S(2)}) copy-start(f32[256]{0:T(256)} %param.9) | copy-start | bytes 3076
  61.6 2.5 %copy-start.3 = (bf16[256,16]{0,1:T(8,128)(2,1)S(1)}, bf16[256,16]{0,1:T(8,128)(2,1)}, u32[]{:S(2)}) copy-start(bf16[256,16]{0,1:T(8,128)(2,1)} %param.11) | copy-start | bytes 24580
  61.6 22.6 %copy-start.4 = (s32[256]{0:T(256)S(1)}, s32[256]{0:T(256)}, u32[]{:S(2)}) copy-start(s32[256]{0:T(256)} %param.13) | copy-start | bytes 3076
  61.6 22.6 %copy-start.5 = (f32[16]{0:T(128)S(1)}, f32[16]{0:T(128)}, u32[]{:S(2)}) copy-start(f32[16]{0:T(128)} %param.12) | copy-start | bytes 196
  64.3 7.5 %collective-permute-start.5 = (f32[256,16]{0,1:T(8,128)S(1)}, f32[256,16]{0,1:T(8,128)S(1)}, u32[]{:S(2)}, u32[]{:S(2)}) collective-permute-start(f32[256,16]{0,1:T(8,128)S(1)} %fusion.5), channel_id=1, source_target_pairs={{0,2},{1,3},{2,0},{3,1},{4,6},{5,7},{6,4},{7,5},{8,10},{9,11},{10,... | collective-permute-start | bytes 49160 | tf_op jit(solution)/shard_map/ppermute | solution.py:18
  71.8 3.7 %collective-permute-start.6 = (f32[256,16]{0,1:T(8,128)S(1)}, f32[256,16]{0,1:T(8,128)S(1)}, u32[]{:S(2)}, u32[]{:S(2)}) collective-permute-start(f32[256,16]{0,1:T(8,128)S(1)} %add.56), channel_id=1, source_target_pairs={{0,1},{1,0},{2,3},{3,2},{4,5},{5,4},{6,7},{7,6},{8,9},{9,8},{10,11... | collective-permute-start | bytes 49160 | tf_op jit(solution)/shard_map/ppermute | solution.py:18
  75.5 3.7 %collective-permute-start.7 = (f32[256,16]{0,1:T(8,128)S(1)}, f32[256,16]{0,1:T(8,128)S(1)}, u32[]{:S(2)}, u32[]{:S(2)}) collective-permute-start(f32[256,16]{0,1:T(8,128)S(1)} %add.57), channel_id=1, source_target_pairs={{0,8},{4,12},{8,0},{12,4},{16,24},{20,28},{24,16},{28,20},{1,9},{5... | collective-permute-start | bytes 49160 | tf_op jit(solution)/shard_map/ppermute | solution.py:18
  79.3 3.7 %collective-permute-start.8 = (f32[256,16]{0,1:T(8,128)S(1)}, f32[256,16]{0,1:T(8,128)S(1)}, u32[]{:S(2)}, u32[]{:S(2)}) collective-permute-start(f32[256,16]{0,1:T(8,128)S(1)} %add.58), channel_id=1, source_target_pairs={{0,16},{4,20},{8,24},{12,28},{16,0},{20,4},{24,8},{28,12},{1,17},{... | collective-permute-start | bytes 49160 | tf_op jit(solution)/shard_map/ppermute | solution.py:18
  83.0 1.2 %collective-permute-start.9 = (f32[256,16]{0,1:T(8,128)S(1)}, f32[256,16]{0,1:T(8,128)S(1)}, u32[]{:S(2)}, u32[]{:S(2)}) collective-permute-start(f32[256,16]{0,1:T(8,128)S(1)} %add.59), channel_id=1, source_target_pairs={{0,4},{4,0},{8,12},{12,8},{16,20},{20,16},{24,28},{28,24},{1,5},{5... | collective-permute-start | bytes 49160 | tf_op jit(solution)/shard_map/ppermute | solution.py:18
